TPU v7x, 512 devices: a whole 4x8x8 slice. The times are simulated.
512 devices in a mesh: rows: 64 (over z, y), feat: 8 (over x, core).
Axes of the slice: x: 4, y: 8, z: 8, core: 2. Of those that a mesh axis runs over, the one named last changes fastest.
Arguments:
- node_feats: bfloat16 [65536, 256], P('rows', 'feat'), may hold values from -6 to 6
- band_weights: bfloat16 [65536, 384], P('rows'), may hold values from 0 to 1.5, as said below
- far_weights: bfloat16 [65536, 256], P('rows'), may hold values from 0 to 1.5, as said below
- far_owner: int32 [512, 2], P('rows'), may hold values from 0 to 63, all different within a row; in each aligned block of 8 rows (0 to 7, 8 to 15, ...) at most 2 rows name the same one
- far_local: int32 [512, 2], P('rows'), may hold values from 0 to 7
- w_self: bfloat16 [256, 256], replicated, may hold values from -0.375 to 0.375
- w_neigh: bfloat16 [256, 256], replicated, may hold values from -0.375 to 0.375
- bias: float32 [256], P('feat'), may hold values from -3 to 3
- cotangent: bfloat16 [65536, 256], P('rows', 'feat'), may hold values from -16 to 16
Outputs:
- layer_out: bfloat16 [65536, 256], P('rows', 'feat')
- grad_feats: float32 [65536, 256], P('rows', 'feat')
- grad_self: float32 [256, 256], P('feat')
- grad_neigh: float32 [256, 256], P('feat')
Inputs may be any that keep to these rules, and one draw needn't show every extreme that they name: `far_owner`: among the far entries of the 8 row blocks of one device, no owner is named more than 2 times, and in every draw some owner is named exactly 2 times in some device's blocks; the 2 owners of one row block differ. `band_weights`: each row has a positive weight on the node's own entry of its own block; other entries are zero or positive. `far_weights`: entries are zero or positive.
All inputs are finite; a program needn't handle non-finite values.
Results may differ from a plain program's by a relative error of at most 0.0049.
Values may be sent and summed in bfloat16 or wider, within the bound.
No kernel may reach another device: no remote copies, remote signals or barrier semaphores. Data moves between devices by JAX's collectives and lax.ppermute only.
A program may use at most 64 MiB of HBM per device.

v0:
```python
import jax
import jax.numpy as jnp
from jax import lax
from jax.sharding import PartitionSpec as P


def extended(block, sides, width):
    for axis, dim in sides:
        count = lax.axis_size(axis)
        forward = [(i, i + 1) for i in range(count - 1)]
        backward = [(target, source) for source, target in forward]
        low = lax.ppermute(
            lax.slice_in_dim(block, block.shape[dim] - width, None, axis=dim), axis, forward
        )
        high = lax.ppermute(lax.slice_in_dim(block, 0, width, axis=dim), axis, backward)
        block = jnp.concatenate([low, block, high], axis=dim)
    return block


def from_behind(block, axis, distance):
    devices = range(lax.axis_size(axis))
    route = [(i - distance, i) for i in devices if i - distance in devices]
    return lax.ppermute(block, axis, route)


def on_device(
    node_feats, band_weights, far_weights, far_owner, far_local, w_self, w_neigh, bias, cotangent
):
    rows_dev, col_count = node_feats.shape
    tile_size = band_weights.shape[1] // 3
    blocks = rows_dev // tile_size
    fanout = far_owner.shape[1]
    peer_count = lax.axis_size("rows")
    capacity = max(2, 2 * blocks * fanout // peer_count)
    col_start = lax.axis_index("feat") * col_count
    padded = extended(node_feats, (("rows", 0),), tile_size)
    windows = jnp.concatenate(
        [
            padded[offset * tile_size : offset * tile_size + rows_dev].reshape(
                blocks, tile_size, col_count
            )
            for offset in range(3)
        ],
        axis=1,
    )
    band_tiles = band_weights.reshape(blocks, tile_size, 3 * tile_size)
    band_sum = jnp.einsum("bij,bjc->bic", band_tiles, windows, preferred_element_type=jnp.float32)
    owner_ids = far_owner.reshape(-1)
    local_ids = far_local.reshape(-1)
    entries = owner_ids.shape[0]
    same_owner = owner_ids[:, None] == owner_ids[None, :]
    earlier = jnp.arange(entries)[None, :] < jnp.arange(entries)[:, None]
    slot_rank = jnp.sum(jnp.where(same_owner & earlier, 1, 0), axis=1).astype(jnp.int32)
    slot_ids = owner_ids * capacity + slot_rank
    slot_hit = slot_ids[:, None] == jnp.arange(peer_count * capacity, dtype=jnp.int32)[None, :]
    request = (jnp.sum(jnp.where(slot_hit, local_ids[:, None] + 1, 0), axis=0) - 1).reshape(
        peer_count, capacity
    )
    wanted = lax.all_to_all(request, "rows", split_axis=0, concat_axis=0, tiled=True)
    usable = wanted >= 0
    safe_ids = jnp.maximum(wanted, 0)
    own_blocks = node_feats.reshape(blocks, tile_size, col_count)
    outgoing = jnp.where(
        usable[:, :, None, None], own_blocks[safe_ids], jnp.zeros((), jnp.bfloat16)
    )
    incoming = lax.all_to_all(outgoing, "rows", split_axis=0, concat_axis=0, tiled=True)
    fetched = incoming.reshape(peer_count * capacity, tile_size, col_count)[slot_ids].reshape(
        blocks, fanout * tile_size, col_count
    )
    far_tiles = far_weights.reshape(blocks, tile_size, fanout * tile_size)
    far_sum = jnp.einsum("bij,bjc->bic", far_tiles, fetched, preferred_element_type=jnp.float32)
    degree = jnp.sum(band_weights.astype(jnp.float32), axis=1) + jnp.sum(
        far_weights.astype(jnp.float32), axis=1
    )
    neighbours = ((band_sum + far_sum).reshape(rows_dev, col_count) / degree[:, None]).astype(
        jnp.bfloat16
    )
    rows_self = lax.dynamic_slice_in_dim(w_self, col_start, col_count, 0)
    rows_neigh = lax.dynamic_slice_in_dim(w_neigh, col_start, col_count, 0)
    terms = jnp.dot(node_feats, rows_self, preferred_element_type=jnp.float32) + jnp.dot(
        neighbours, rows_neigh, preferred_element_type=jnp.float32
    )
    preact = lax.psum_scatter(terms, "feat", scatter_dimension=1, tiled=True)
    preact = preact + bias
    layer_out = jax.nn.silu(preact).astype(jnp.bfloat16)
    sigmoid_z = jax.nn.sigmoid(preact)
    grad_pre = (
        cotangent.astype(jnp.float32) * sigmoid_z * (1.0 + preact * (1.0 - sigmoid_z))
    ).astype(jnp.bfloat16)
    full_grad = lax.all_gather(grad_pre, "feat", axis=1, tiled=True)
    grad_scale = float(rows_dev * peer_count) ** (-0.5)
    part_self = jnp.einsum("rc,rf->cf", node_feats, full_grad, preferred_element_type=jnp.float32)
    part_neigh = jnp.einsum("rc,rf->cf", neighbours, full_grad, preferred_element_type=jnp.float32)
    sum_self, sum_neigh = lax.psum((part_self, part_neigh), "rows")
    grad_self = sum_self * grad_scale
    grad_neigh = sum_neigh * grad_scale
    dense_grad = jnp.einsum("rf,cf->rc", full_grad, rows_self, preferred_element_type=jnp.float32)
    grad_agg = jnp.einsum("rf,cf->rc", full_grad, rows_neigh, preferred_element_type=jnp.float32)
    grad_neighbours = (grad_agg / degree[:, None]).astype(jnp.bfloat16)
    grad_blocks = grad_neighbours.reshape(blocks, tile_size, col_count)
    grad_windows = jnp.einsum(
        "bij,bic->bjc", band_tiles, grad_blocks, preferred_element_type=jnp.float32
    )
    grad_padded = jnp.zeros((rows_dev + 2 * tile_size, col_count), jnp.float32)
    for offset in range(3):
        piece = grad_windows[:, offset * tile_size : (offset + 1) * tile_size, :].reshape(
            rows_dev, col_count
        )
        grad_padded = grad_padded + jnp.pad(
            piece, ((offset * tile_size, (2 - offset) * tile_size), (0, 0))
        )
    top_rim = grad_padded[:tile_size]
    bottom_rim = grad_padded[rows_dev + tile_size :]
    from_below = from_behind(top_rim, "rows", -1)
    from_above = from_behind(bottom_rim, "rows", 1)
    grad_fetched = jnp.einsum(
        "bij,bic->bjc", far_tiles, grad_blocks, preferred_element_type=jnp.float32
    )
    returning = jnp.zeros((peer_count * capacity, tile_size, col_count), jnp.float32)
    returning = returning.at[slot_ids].set(grad_fetched.reshape(entries, tile_size, col_count))
    returned = lax.all_to_all(
        returning.reshape(peer_count, capacity, tile_size, col_count).astype(jnp.bfloat16),
        "rows",
        split_axis=0,
        concat_axis=0,
        tiled=True,
    ).astype(jnp.float32)
    target_block = jnp.where(usable, wanted, blocks).reshape(-1)
    owed = jnp.zeros((blocks, tile_size * col_count), jnp.float32)
    owed = owed.at[target_block].add(
        returned.reshape(peer_count * capacity, tile_size * col_count), mode="drop"
    )
    interior = (
        dense_grad
        + grad_padded[tile_size : tile_size + rows_dev]
        + owed.reshape(rows_dev, col_count)
    )
    interior = interior.at[:tile_size].add(from_above)
    grad_feats = interior.at[rows_dev - tile_size :].add(from_below)
    return (layer_out, grad_feats, grad_self, grad_neigh)


def solution(mesh):
    in_specs = (
        P("rows", "feat"),
        P("rows", None),
        P("rows", None),
        P("rows", None),
        P("rows", None),
        P(),
        P(),
        P("feat"),
        P("rows", "feat"),
    )
    out_specs = (P("rows", "feat"), P("rows", "feat"), P("feat", None), P("feat", None))
    return jax.shard_map(
        on_device, mesh=mesh, in_specs=in_specs, out_specs=out_specs, check_vma=False
    )
```

profile of v0, /device:TPU:2, one launch (start us, length us, event | category | flops | bytes accessed | tf_op | source)
XLA Modules:
  0.0 326.7 jit_solution(16754911278057413692)
XLA Ops:
  10.0 16.6 %all-to-all-start = ((s32[64,1,2]{2,1,0:T(1,128)}), s32[64,1,2]{2,1,0:T(1,128)S(1)}, u32[]{:S(2)}, u32[]{:S(2)}) async-start(s32[64,1,2]{2,1,0:T(1,128)} %bitcast.2), calls=%async_computation | async-start | bytes 65536 | tf_op jit(solution)/shard_map/all_to_all | solution.py:59
  26.5 0.9 copy_bitcast_fusion.4
  27.4 11.1 %all-to-all-done = s32[64,1,2]{2,1,0:T(1,128)S(1)} async-done(((s32[64,1,2]{2,1,0:T(1,128)}), s32[64,1,2]{2,1,0:T(1,128)S(1)}, u32[]{:S(2)}, u32[]{:S(2)}) %all-to-all-start) | async-done | bytes 544 | tf_op jit(solution)/shard_map/all_to_all | solution.py:59
  39.0 1.4 fusion.37
  41.6 1.2 broadcast_select_fusion
  42.8 5.5 %all-to-all-start.1 = ((bf16[64,2,128,32]{2,3,1,0:T(8,128)(2,1)}), bf16[64,2,128,32]{2,3,1,0:T(8,128)(2,1)}, u32[]{:S(2)}, u32[]{:S(2)}) async-start(bf16[64,2,128,32]{2,3,1,0:T(8,128)(2,1)} %broadcast_select_fusion), calls=%async_computation.1 | async-start | bytes 2097152 | tf_op jit(solution)/shard_map/all_to_all | solution.py:66
  48.4 3.3 %collective-permute-start = (bf16[128,32]{0,1:T(8,128)(2,1)S(1)}, bf16[128,32]{0,1:T(8,128)(2,1)S(1)}, u32[]{:S(2)}, u32[]{:S(2)}) collective-permute-start(bf16[128,32]{0,1:T(8,128)(2,1)S(1)} %get-tuple-element.41), channel_id=1, source_target_pairs={{0,8},{8,16},{16,24},{24,32},{32,40},{40,48},{48,56},{56,64},{64,7... | collective-permute-start | bytes 24584 | tf_op jit(solution)/shard_map/ppermute | solution.py:12
  51.7 1.3 collective-permute-start.1
  53.7 1.0 convolution_bitcast_fusion
  54.7 13.0 %collective-permute-done = bf16[128,32]{0,1:T(8,128)(2,1)S(1)} collective-permute-done((bf16[128,32]{0,1:T(8,128)(2,1)S(1)}, bf16[128,32]{0,1:T(8,128)(2,1)S(1)}, u32[]{:S(2)}, u32[]{:S(2)}) %collective-permute-start) | collective-permute-done | bytes 8224 | tf_op jit(solution)/shard_map/ppermute | solution.py:12
  67.7 3.3 %collective-permute-done.1 = bf16[128,32]{0,1:T(8,128)(2,1)S(1)} collective-permute-done((bf16[128,32]{0,1:T(8,128)(2,1)S(1)}, bf16[128,32]{0,1:T(8,128)(2,1)S(1)}, u32[]{:S(2)}, u32[]{:S(2)}) %collective-permute-start.1) | collective-permute-done | bytes 8224 | tf_op jit(solution)/shard_map/ppermute | solution.py:15
  71.4 5.6 %all-to-all-done.1 = bf16[64,2,128,32]{2,3,1,0:T(8,128)(2,1)} async-done(((bf16[64,2,128,32]{2,3,1,0:T(8,128)(2,1)}), bf16[64,2,128,32]{2,3,1,0:T(8,128)(2,1)}, u32[]{:S(2)}, u32[]{:S(2)}) %all-to-all-start.1) | async-done | bytes 1048608 | tf_op jit(solution)/shard_map/all_to_all | solution.py:66
  77.0 1.8 gather_fusion.1
  79.2 1.3 convolution_add_fusion
  80.5 28.6 %reduce-scatter.2.cloned.1.call-done = f32[1024,32]{0,1:T(8,128)} async-done(((f32[1024,256]{0,1:T(8,128)}), f32[1024,32]{0,1:T(8,128)}) %reduce-scatter.2.cloned.1.call-update) | async-done | bytes 131088 | tf_op jit(solution)/shard_map/reduce_scatter | solution.py:83
  109.2 1.7 multiply_convert_fusion
  110.8 13.8 %all_gather.3 = bf16[1024,256]{0,1:T(8,128)(2,1)S(1)} all-gather(bf16[1024,32]{0,1:T(8,128)(2,1)S(1)} %get-tuple-element.37), channel_id=1, replica_groups=mesh['rows'=64,'feat'=8] {'feat'}, dimensions={1}, use_global_device_ids=true | all-gather | bytes 589824 | tf_op jit(solution)/shard_map/all_gather | solution.py:90
  126.0 1.0 scatter_fusion
  127.1 1.2 convert_element_type.41
  128.3 13.3 %all-to-all-start.2 = ((bf16[64,2,128,32]{2,3,1,0:T(8,128)(2,1)}), bf16[64,2,128,32]{2,3,1,0:T(8,128)(2,1)S(1)}, u32[]{:S(2)}, u32[]{:S(2)}) async-start(bf16[64,2,128,32]{2,3,1,0:T(8,128)(2,1)} %bitcast.88), calls=%async_computation.3 | async-start | bytes 2097152 | tf_op jit(solution)/shard_map/all_to_all | solution.py:121
  142.1 0.9 convolution_bitcast_fusion.3
  143.0 0.9 fusion.34
  144.0 3.5 %collective-permute-start.2 = (f32[128,32]{0,1:T(8,128)S(1)}, f32[128,32]{0,1:T(8,128)S(1)}, u32[]{:S(2)}, u32[]{:S(2)}) collective-permute-start(f32[128,32]{0,1:T(8,128)S(1)} %get-tuple-element.33), channel_id=1, source_target_pairs={{0,8},{8,16},{16,24},{24,32},{32,40},{40,48},{48,56},{56,64},{64,7... | collective-permute-start | bytes 49160 | tf_op jit(solution)/shard_map/ppermute | solution.py:23
  147.5 1.5 collective-permute-start.3
  148.9 151.1 %all-reduce.6.cloned.1.call-done = (f32[32,256]{1,0:T(8,128)}, f32[32,256]{1,0:T(8,128)}) async-done(((f32[32,256]{1,0:T(8,128)}, f32[32,256]{1,0:T(8,128)}), (f32[32,256]{1,0:T(8,128)}, f32[32,256]{1,0:T(8,128)})) %all-reduce.6.cloned.1.call-update) | async-done | bytes 65552 | tf_op jit(solution)/shard_map/psum | solution.py:94
  300.0 1.4 broadcast_multiply_fusion.1
  301.4 1.4 broadcast_multiply_fusion
  302.8 4.1 %copy.105 = f32[64,2,128,32]{3,2,1,0:T(8,128)} copy(bf16[64,2,128,32]{2,3,1,0:T(8,128)(2,1)S(1)} %all-to-all-done.2) | data formatting | bytes 3145728 | tf_op jit(solution)/shard_map/reshape | solution.py:131
  306.9 6.2 %reshape.273 = f32[128,4096]{1,0:T(8,128)S(1)} reshape(f32[64,2,128,32]{3,2,1,0:T(8,128)} %copy.105) | data formatting | bytes 4194304 | tf_op jit(solution)/shard_map/reshape | solution.py:131
  313.1 3.8 %scatter_custom_fusion.1 = f32[8,4096]{1,0:T(8,128)} fusion(s32[128]{0:T(128)S(1)} %fusion.32, f32[128,4096]{1,0:T(8,128)S(1)} %reshape.273, f32[]{:T(128)} %constant.91.clone.1), kind=kCustom, calls=%fused_computation.47 | custom fusion | flops 524288 | bytes 131076 | tf_op jit(solution)/shard_map/scatter-add | solution.py:130
  316.9 1.1 reshape.242
  318.2 0.9 fusion
  (79 shorter events, 8.7 us)
Async XLA Ops:
  7.2 72.0 %copy-start = (bf16[256,256]{1,0:T(8,128)(2,1)S(1)}, bf16[256,256]{1,0:T(8,128)(2,1)}, u32[]{:S(2)}) copy-start(bf16[256,256]{1,0:T(8,128)(2,1)} %param.19) | copy-start | bytes 393220
  10.0 28.5 %all-to-all-start = ((s32[64,1,2]{2,1,0:T(1,128)}), s32[64,1,2]{2,1,0:T(1,128)S(1)}, u32[]{:S(2)}, u32[]{:S(2)}) async-start(s32[64,1,2]{2,1,0:T(1,128)} %bitcast.2), calls=%async_computation | async-start | bytes 65536 | tf_op jit(solution)/shard_map/all_to_all | solution.py:59
  41.5 6.9 %copy-start.5 = (bf16[1024,32]{0,1:T(8,128)(2,1)S(1)}, bf16[1024,32]{0,1:T(8,128)(2,1)}, u32[]{:S(2)}) copy-start(bf16[1024,32]{0,1:T(8,128)(2,1)} %param.13) | copy-start | bytes 196612
  41.5 11.5 %copy-start.9 = (s32[8,2]{0,1:T(2,128)S(1)}, s32[8,2]{0,1:T(2,128)}, u32[]{:S(2)}) copy-start(s32[8,2]{0,1:T(2,128)} %param.16) | copy-start | bytes 196
  41.6 11.6 %copy-start.2 = (bf16[1024,256]{1,0:T(8,128)(2,1)S(1)}, bf16[1024,256]{1,0:T(8,128)(2,1)}, u32[]{:S(2)}) copy-start(bf16[1024,256]{1,0:T(8,128)(2,1)} %param.15) | copy-start | bytes 1572868
  41.6 11.9 %copy-start.1 = (bf16[1024,384]{1,0:T(8,128)(2,1)S(1)}, bf16[1024,384]{1,0:T(8,128)(2,1)}, u32[]{:S(2)}) copy-start(bf16[1024,384]{1,0:T(8,128)(2,1)} %param.14) | copy-start | bytes 2359300
  42.8 34.2 %all-to-all-start.1 = ((bf16[64,2,128,32]{2,3,1,0:T(8,128)(2,1)}), bf16[64,2,128,32]{2,3,1,0:T(8,128)(2,1)}, u32[]{:S(2)}, u32[]{:S(2)}) async-start(bf16[64,2,128,32]{2,3,1,0:T(8,128)(2,1)} %broadcast_select_fusion), calls=%async_computation.1 | async-start | bytes 2097152 | tf_op jit(solution)/shard_map/all_to_all | solution.py:66
  48.3 60.8 %reduce-scatter.2.cloned.1.call-start = ((), (), s32[]{:S(2)}) async-start(), calls=%async_computation.4 | async-start | bytes 1179648 | tf_op jit(solution)/shard_map/reduce_scatter | solution.py:83
  48.4 19.3 %collective-permute-start = (bf16[128,32]{0,1:T(8,128)(2,1)S(1)}, bf16[128,32]{0,1:T(8,128)(2,1)S(1)}, u32[]{:S(2)}, u32[]{:S(2)}) collective-permute-start(bf16[128,32]{0,1:T(8,128)(2,1)S(1)} %get-tuple-element.41), channel_id=1, source_target_pairs={{0,8},{8,16},{16,24},{24,32},{32,40},{40,48},{48,56},{56,64},{64,7... | collective-permute-start | bytes 24584 | tf_op jit(solution)/shard_map/ppermute | solution.py:12
  51.7 19.3 %collective-permute-start.1 = (bf16[128,32]{0,1:T(8,128)(2,1)S(1)}, bf16[128,32]{0,1:T(8,128)(2,1)S(1)}, u32[]{:S(2)}, u32[]{:S(2)}) collective-permute-start(bf16[128,32]{0,1:T(8,128)(2,1)S(1)} %get-tuple-element.42), channel_id=1, source_target_pairs={{8,0},{16,8},{24,16},{32,24},{40,32},{48,40},{56,48},{64,56},{72,6... | collective-permute-start | bytes 24584 | tf_op jit(solution)/shard_map/ppermute | solution.py:15
  78.9 30.3 %copy-start.8 = (bf16[1024,32]{0,1:T(8,128)(2,1)S(1)}, bf16[1024,32]{0,1:T(8,128)(2,1)}, u32[]{:S(2)}) copy-start(bf16[1024,32]{0,1:T(8,128)(2,1)} %param.21) | copy-start | bytes 196612
  78.9 30.2 %copy-start.10 = (f32[32]{0:T(128)S(1)}, f32[32]{0:T(128)}, u32[]{:S(2)}) copy-start(f32[32]{0:T(128)} %param.20) | copy-start | bytes 388
  124.7 0.8 copy-start.3
  127.1 14.5 %copy-start.7 = (s32[64,2]{1,0:T(8,128)S(1)}, s32[64,2]{1,0:T(8,128)}, u32[]{:S(2)}) copy-start(s32[64,2]{1,0:T(8,128)} %get-tuple-element.28) | copy-start | bytes 1540
  128.3 13.9 %copy-start.4 = (bf16[1024,256]{0,1:T(8,128)(2,1)S(1)}, bf16[1024,256]{0,1:T(8,128)(2,1)}, u32[]{:S(2)}) copy-start(bf16[1024,256]{0,1:T(8,128)(2,1)} %copy-done.3) | copy-start | bytes 1572868
  128.3 174.5 %all-to-all-start.2 = ((bf16[64,2,128,32]{2,3,1,0:T(8,128)(2,1)}), bf16[64,2,128,32]{2,3,1,0:T(8,128)(2,1)S(1)}, u32[]{:S(2)}, u32[]{:S(2)}) async-start(bf16[64,2,128,32]{2,3,1,0:T(8,128)(2,1)} %bitcast.88), calls=%async_computation.3 | async-start | bytes 2097152 | tf_op jit(solution)/shard_map/all_to_all | solution.py:121
  141.6 158.5 %all-reduce.6.cloned.1.call-start = ((), (), s32[]{:S(2)}) async-start(), calls=%async_computation.5 | async-start | bytes 131072 | tf_op jit(solution)/shard_map/psum | solution.py:94
  144.0 175.1 %collective-permute-start.2 = (f32[128,32]{0,1:T(8,128)S(1)}, f32[128,32]{0,1:T(8,128)S(1)}, u32[]{:S(2)}, u32[]{:S(2)}) collective-permute-start(f32[128,32]{0,1:T(8,128)S(1)} %get-tuple-element.33), channel_id=1, source_target_pairs={{0,8},{8,16},{16,24},{24,32},{32,40},{40,48},{48,56},{56,64},{64,7... | collective-permute-start | bytes 49160 | tf_op jit(solution)/shard_map/ppermute | solution.py:23
  147.5 171.7 %collective-permute-start.3 = (f32[128,32]{0,1:T(8,128)S(1)}, f32[128,32]{0,1:T(8,128)S(1)}, u32[]{:S(2)}, u32[]{:S(2)}) collective-permute-start(f32[128,32]{0,1:T(8,128)S(1)} %get-tuple-element.32), channel_id=1, source_target_pairs={{8,0},{16,8},{24,16},{32,24},{40,32},{48,40},{56,48},{64,56},{72,6... | collective-permute-start | bytes 49160 | tf_op jit(solution)/shard_map/ppermute | solution.py:23
  319.2 0.7 copy-start.6
Sparse Core Ops, SparseCore 0:
  80.7 28.4 reduce-scatter.1
  146.3 153.6 all-reduce.5
where the time goes:
time: 328 us; the launch traced here: 327 us
  waiting for transfers between devices  213 us (65%)
  starting transfers between devices  45 us (14%)
  local copies, waits for them, and re-layouts  20.8 us (6%)
  between operations  14.5 us (4%)
  blocking collectives  13.8 us (4%)
  other arithmetic  13.6 us (4%)
  matrix products  6.33 us (2%)
    psum x1, waiting for transfers between devices, on_device(): sum_self, sum_neigh = lax.psum((part_self, part_neigh), 'rows')  151 us
    reduce_scatter x1, waiting for transfers between devices, on_device(): preact = lax.psum_scatter(terms, 'feat', scatter_dimension=1, tiled=True)  28.6 us
    all_to_all x1, starting transfers between devices, on_device(): lax.all_to_all(request, 'rows', split_axis=0, concat_axis=0, tiled=True)  16.6 us
    all_gather x1, blocking collectives, on_device(): full_grad = lax.all_gather(grad_pre, 'feat', axis=1, tiled=True)  13.8 us
    all_to_all x1, starting transfers between devices, on_device(): lax.all_to_all(returning.reshape(peer_count, capacity, tile_size, col_cou...  13.3 us
    ppermute x1, waiting for transfers between devices, extended(): lax.ppermute(lax.slice_in_dim(block, block.shape[dim] - width, None, axis...  13 us
    all_to_all x1, waiting for transfers between devices, on_device(): lax.all_to_all(request, 'rows', split_axis=0, concat_axis=0, tiled=True)  11.1 us
    reshape x2, local copies, waits for them, and re-layouts, on_device(): returned.reshape(peer_count * capacity, tile_size * col_count)  10.3 us
  transfers between devices with their start and end apart: 9, of which 6 were waited for; matrix products, arithmetic and copies ran while one was open for 7% of the time, Pallas kernels for 0%

commit v1 on v0

--- a/solution.py
+++ b/solution.py
@@ -87,7 +87,8 @@
     grad_pre = (
         cotangent.astype(jnp.float32) * sigmoid_z * (1.0 + preact * (1.0 - sigmoid_z))
     ).astype(jnp.bfloat16)
-    full_grad = lax.all_gather(grad_pre, "feat", axis=1, tiled=True)
+    copies = jnp.concatenate([grad_pre] * lax.axis_size("feat"), axis=1)
+    full_grad = lax.all_to_all(copies, "feat", 1, 1, tiled=True)
     grad_scale = float(rows_dev * peer_count) ** (-0.5)
     part_self = jnp.einsum("rc,rf->cf", node_feats, full_grad, preferred_element_type=jnp.float32)
     part_neigh = jnp.einsum("rc,rf->cf", neighbours, full_grad, preferred_element_type=jnp.float32)

time: 328 us -> 329 us (level)
  blocking collectives: 13.8 us -> 0 us
  starting transfers between devices: 45 us -> 52.2 us
  local copies, waits for them, and re-layouts: 20.8 us -> 24.9 us
    all_gather x1 -> x0, blocking collectives: 13.8 us -> none  [on_device(): full_grad = lax.all_gather(grad_pre, 'feat', axis=1, tiled=True)]
    all_to_all x0 -> x1, waiting for transfers between devices: none -> 8.78 us  [on_device(): full_grad = lax.all_to_all(copies, 'feat', 1, 1, tiled=True)]
    all_to_all x0 -> x1, starting transfers between devices: none -> 7.01 us  [on_device(): full_grad = lax.all_to_all(copies, 'feat', 1, 1, tiled=True)]
    psum x1, waiting for transfers between devices: 151 us -> 146 us  [on_device(): sum_self, sum_neigh = lax.psum((part_self, part_neigh), 'rows')]
    unnamed x24 -> x30, local copies, waits for them, and re-layouts: 1.92 us -> 5.48 us
  transfers between devices with their start and end apart: 9 -> 10, of which waited for: 6 -> 7; matrix products, arithmetic and copies ran while one was open for 7% -> 8% of each run, Pallas kernels for 0% -> 0%
where the time goes in v1:
time: 329 us; the launch traced here: 328 us
  waiting for transfers between devices  216 us (66%)
  starting transfers between devices  52.2 us (16%)
  local copies, waits for them, and re-layouts  24.9 us (8%)
  between operations  14.5 us (4%)
  other arithmetic  13.8 us (4%)
  matrix products  6.31 us (2%)
    psum x1, waiting for transfers between devices, on_device(): sum_self, sum_neigh = lax.psum((part_self, part_neigh), 'rows')  146 us
    reduce_scatter x1, waiting for transfers between devices, on_device(): preact = lax.psum_scatter(terms, 'feat', scatter_dimension=1, tiled=True)  28.5 us
    all_to_all x1, starting transfers between devices, on_device(): lax.all_to_all(request, 'rows', split_axis=0, concat_axis=0, tiled=True)  16.6 us
    all_to_all x1, starting transfers between devices, on_device(): lax.all_to_all(returning.reshape(peer_count, capacity, tile_size, col_cou...  13.5 us
    ppermute x1, waiting for transfers between devices, extended(): lax.ppermute(lax.slice_in_dim(block, block.shape[dim] - width, None, axis...  13 us
    all_to_all x1, waiting for transfers between devices, on_device(): lax.all_to_all(request, 'rows', split_axis=0, concat_axis=0, tiled=True)  11.1 us
    reshape x2, local copies, waits for them, and re-layouts, on_device(): returned.reshape(peer_count * capacity, tile_size * col_count)  10.3 us
    all_to_all x1, waiting for transfers between devices, on_device(): full_grad = lax.all_to_all(copies, 'feat', 1, 1, tiled=True)  8.78 us
  transfers between devices with their start and end apart: 10, of which 7 were waited for; matrix products, arithmetic and copies ran while one was open for 8% of the time, Pallas kernels for 0%

profile of v1, /device:TPU:2, one launch (start us, length us, event | category | flops | bytes accessed | tf_op | source)
XLA Modules:
  0.0 328.0 jit_solution(11901654825612508072)
XLA Ops:
  10.0 16.6 %all-to-all-start = ((s32[64,1,2]{2,1,0:T(1,128)}), s32[64,1,2]{2,1,0:T(1,128)S(1)}, u32[]{:S(2)}, u32[]{:S(2)}) async-start(s32[64,1,2]{2,1,0:T(1,128)} %bitcast.2), calls=%async_computation | async-start | bytes 65536 | tf_op jit(solution)/shard_map/all_to_all | solution.py:59
  26.5 0.9 copy_bitcast_fusion.4
  27.4 11.1 %all-to-all-done = s32[64,1,2]{2,1,0:T(1,128)S(1)} async-done(((s32[64,1,2]{2,1,0:T(1,128)}), s32[64,1,2]{2,1,0:T(1,128)S(1)}, u32[]{:S(2)}, u32[]{:S(2)}) %all-to-all-start) | async-done | bytes 544 | tf_op jit(solution)/shard_map/all_to_all | solution.py:59
  41.0 1.2 broadcast_select_fusion
  42.3 5.5 %all-to-all-start.1 = ((bf16[64,2,128,32]{2,3,1,0:T(8,128)(2,1)}), bf16[64,2,128,32]{2,3,1,0:T(8,128)(2,1)}, u32[]{:S(2)}, u32[]{:S(2)}) async-start(bf16[64,2,128,32]{2,3,1,0:T(8,128)(2,1)} %broadcast_select_fusion), calls=%async_computation.1 | async-start | bytes 2097152 | tf_op jit(solution)/shard_map/all_to_all | solution.py:66
  47.9 3.3 %collective-permute-start = (bf16[128,32]{0,1:T(8,128)(2,1)S(1)}, bf16[128,32]{0,1:T(8,128)(2,1)S(1)}, u32[]{:S(2)}, u32[]{:S(2)}) collective-permute-start(bf16[128,32]{0,1:T(8,128)(2,1)S(1)} %get-tuple-element.41), channel_id=1, source_target_pairs={{0,8},{8,16},{16,24},{24,32},{32,40},{40,48},{48,56},{56,64},{64,7... | collective-permute-start | bytes 24584 | tf_op jit(solution)/shard_map/ppermute | solution.py:12
  51.2 1.3 collective-permute-start.1
  53.1 1.0 convolution_bitcast_fusion
  54.2 13.0 %collective-permute-done = bf16[128,32]{0,1:T(8,128)(2,1)S(1)} collective-permute-done((bf16[128,32]{0,1:T(8,128)(2,1)S(1)}, bf16[128,32]{0,1:T(8,128)(2,1)S(1)}, u32[]{:S(2)}, u32[]{:S(2)}) %collective-permute-start) | collective-permute-done | bytes 8224 | tf_op jit(solution)/shard_map/ppermute | solution.py:12
  67.2 3.3 collective-permute-done.1
  70.9 5.6 %all-to-all-done.1 = bf16[64,2,128,32]{2,3,1,0:T(8,128)(2,1)} async-done(((bf16[64,2,128,32]{2,3,1,0:T(8,128)(2,1)}), bf16[64,2,128,32]{2,3,1,0:T(8,128)(2,1)}, u32[]{:S(2)}, u32[]{:S(2)}) %all-to-all-start.1) | async-done | bytes 1048608 | tf_op jit(solution)/shard_map/all_to_all | solution.py:66
  76.4 1.8 gather_fusion.1
  78.7 1.3 convolution_add_fusion
  80.0 28.5 %reduce-scatter.2.cloned.1.call-done = f32[1024,32]{0,1:T(8,128)} async-done(((f32[1024,256]{0,1:T(8,128)}), f32[1024,32]{0,1:T(8,128)}) %reduce-scatter.2.cloned.1.call-update) | async-done | bytes 131088 | tf_op jit(solution)/shard_map/reduce_scatter | solution.py:83
  108.5 1.7 constant_dynamic-update-slice_fusion.7
  114.6 7.0 %all-to-all-start.2 = ((bf16[1024,8,32]{0,2,1:T(8,128)(2,1)}), bf16[1024,8,32]{0,2,1:T(8,128)(2,1)S(1)}, u32[]{:S(2)}, u32[]{:S(2)}) async-start(bf16[1024,8,32]{0,2,1:T(8,128)(2,1)} %bitcast.10), calls=%async_computation.3 | async-start | bytes 1048576 | tf_op jit(solution)/shard_map/all_to_all | solution.py:91
  121.7 8.8 %all-to-all-done.2 = bf16[1024,8,32]{0,2,1:T(8,128)(2,1)S(1)} async-done(((bf16[1024,8,32]{0,2,1:T(8,128)(2,1)}), bf16[1024,8,32]{0,2,1:T(8,128)(2,1)S(1)}, u32[]{:S(2)}, u32[]{:S(2)}) %all-to-all-start.2) | async-done | bytes 524320 | tf_op jit(solution)/shard_map/all_to_all | solution.py:91
  131.7 1.0 scatter_fusion
  132.7 1.2 convert_element_type.46
  133.9 13.5 %all-to-all-start.3 = ((bf16[64,2,128,32]{2,3,1,0:T(8,128)(2,1)}), bf16[64,2,128,32]{2,3,1,0:T(8,128)(2,1)S(1)}, u32[]{:S(2)}, u32[]{:S(2)}) async-start(bf16[64,2,128,32]{2,3,1,0:T(8,128)(2,1)} %bitcast.110), calls=%async_computation.4 | async-start | bytes 2097152 | tf_op jit(solution)/shard_map/all_to_all | solution.py:122
  148.6 0.9 convolution_bitcast_fusion.3
  149.5 0.9 fusion.13
  150.4 3.5 %collective-permute-start.2 = (f32[128,32]{0,1:T(8,128)S(1)}, f32[128,32]{0,1:T(8,128)S(1)}, u32[]{:S(2)}, u32[]{:S(2)}) collective-permute-start(f32[128,32]{0,1:T(8,128)S(1)} %get-tuple-element.35), channel_id=1, source_target_pairs={{0,8},{8,16},{16,24},{24,32},{32,40},{40,48},{48,56},{56,64},{64,7... | collective-permute-start | bytes 49160 | tf_op jit(solution)/shard_map/ppermute | solution.py:23
  153.9 1.5 collective-permute-start.3
  155.4 146.0 %all-reduce.6.cloned.1.call-done = (f32[32,256]{1,0:T(8,128)}, f32[32,256]{1,0:T(8,128)}) async-done(((f32[32,256]{1,0:T(8,128)}, f32[32,256]{1,0:T(8,128)}), (f32[32,256]{1,0:T(8,128)}, f32[32,256]{1,0:T(8,128)})) %all-reduce.6.cloned.1.call-update) | async-done | bytes 65552 | tf_op jit(solution)/shard_map/psum | solution.py:95
  301.4 1.4 broadcast_multiply_fusion.1
  302.7 1.4 broadcast_multiply_fusion
  304.1 4.1 %copy.108 = f32[64,2,128,32]{3,2,1,0:T(8,128)} copy(bf16[64,2,128,32]{2,3,1,0:T(8,128)(2,1)S(1)} %all-to-all-done.3) | data formatting | bytes 3145728 | tf_op jit(solution)/shard_map/reshape | solution.py:132
  308.2 6.2 %reshape.284 = f32[128,4096]{1,0:T(8,128)S(1)} reshape(f32[64,2,128,32]{3,2,1,0:T(8,128)} %copy.108) | data formatting | bytes 4194304 | tf_op jit(solution)/shard_map/reshape | solution.py:132
  314.4 3.8 %scatter_custom_fusion.1 = f32[8,4096]{1,0:T(8,128)} fusion(s32[128]{0:T(128)S(1)} %fusion.38, f32[128,4096]{1,0:T(8,128)S(1)} %reshape.284, f32[]{:T(128)} %constant.91.clone.1), kind=kCustom, calls=%fused_computation.51 | custom fusion | flops 524288 | bytes 131076 | tf_op jit(solution)/shard_map/scatter-add | solution.py:131
  318.2 1.1 reshape.253
  319.5 0.9 fusion
  (88 shorter events, 14.4 us)
Async XLA Ops:
  7.2 71.5 %copy-start = (bf16[256,256]{1,0:T(8,128)(2,1)S(1)}, bf16[256,256]{1,0:T(8,128)(2,1)}, u32[]{:S(2)}) copy-start(bf16[256,256]{1,0:T(8,128)(2,1)} %param.19) | copy-start | bytes 393220
  10.0 28.5 %all-to-all-start = ((s32[64,1,2]{2,1,0:T(1,128)}), s32[64,1,2]{2,1,0:T(1,128)S(1)}, u32[]{:S(2)}, u32[]{:S(2)}) async-start(s32[64,1,2]{2,1,0:T(1,128)} %bitcast.2), calls=%async_computation | async-start | bytes 65536 | tf_op jit(solution)/shard_map/all_to_all | solution.py:59
  41.0 6.9 %copy-start.5 = (bf16[1024,32]{0,1:T(8,128)(2,1)S(1)}, bf16[1024,32]{0,1:T(8,128)(2,1)}, u32[]{:S(2)}) copy-start(bf16[1024,32]{0,1:T(8,128)(2,1)} %param.13) | copy-start | bytes 196612
  41.0 11.5 %copy-start.9 = (s32[8,2]{0,1:T(2,128)S(1)}, s32[8,2]{0,1:T(2,128)}, u32[]{:S(2)}) copy-start(s32[8,2]{0,1:T(2,128)} %param.16) | copy-start | bytes 196
  41.0 11.6 %copy-start.2 = (bf16[1024,256]{1,0:T(8,128)(2,1)S(1)}, bf16[1024,256]{1,0:T(8,128)(2,1)}, u32[]{:S(2)}) copy-start(bf16[1024,256]{1,0:T(8,128)(2,1)} %param.15) | copy-start | bytes 1572868
  41.0 11.8 %copy-start.1 = (bf16[1024,384]{1,0:T(8,128)(2,1)S(1)}, bf16[1024,384]{1,0:T(8,128)(2,1)}, u32[]{:S(2)}) copy-start(bf16[1024,384]{1,0:T(8,128)(2,1)} %param.14) | copy-start | bytes 2359300
  42.3 34.2 %all-to-all-start.1 = ((bf16[64,2,128,32]{2,3,1,0:T(8,128)(2,1)}), bf16[64,2,128,32]{2,3,1,0:T(8,128)(2,1)}, u32[]{:S(2)}, u32[]{:S(2)}) async-start(bf16[64,2,128,32]{2,3,1,0:T(8,128)(2,1)} %broadcast_select_fusion), calls=%async_computation.1 | async-start | bytes 2097152 | tf_op jit(solution)/shard_map/all_to_all | solution.py:66
  47.8 60.8 %reduce-scatter.2.cloned.1.call-start = ((), (), s32[]{:S(2)}) async-start(), calls=%async_computation.5 | async-start | bytes 1179648 | tf_op jit(solution)/shard_map/reduce_scatter | solution.py:83
  47.9 19.3 %collective-permute-start = (bf16[128,32]{0,1:T(8,128)(2,1)S(1)}, bf16[128,32]{0,1:T(8,128)(2,1)S(1)}, u32[]{:S(2)}, u32[]{:S(2)}) collective-permute-start(bf16[128,32]{0,1:T(8,128)(2,1)S(1)} %get-tuple-element.41), channel_id=1, source_target_pairs={{0,8},{8,16},{16,24},{24,32},{32,40},{40,48},{48,56},{56,64},{64,7... | collective-permute-start | bytes 24584 | tf_op jit(solution)/shard_map/ppermute | solution.py:12
  51.2 19.3 %collective-permute-start.1 = (bf16[128,32]{0,1:T(8,128)(2,1)S(1)}, bf16[128,32]{0,1:T(8,128)(2,1)S(1)}, u32[]{:S(2)}, u32[]{:S(2)}) collective-permute-start(bf16[128,32]{0,1:T(8,128)(2,1)S(1)} %get-tuple-element.42), channel_id=1, source_target_pairs={{8,0},{16,8},{24,16},{32,24},{40,32},{48,40},{56,48},{64,56},{72,6... | collective-permute-start | bytes 24584 | tf_op jit(solution)/shard_map/ppermute | solution.py:15
  78.3 30.2 %copy-start.8 = (bf16[1024,32]{0,1:T(8,128)(2,1)S(1)}, bf16[1024,32]{0,1:T(8,128)(2,1)}, u32[]{:S(2)}) copy-start(bf16[1024,32]{0,1:T(8,128)(2,1)} %param.21) | copy-start | bytes 196612
  78.4 30.2 %copy-start.10 = (f32[32]{0:T(128)S(1)}, f32[32]{0:T(128)}, u32[]{:S(2)}) copy-start(f32[32]{0:T(128)} %param.20) | copy-start | bytes 388
  114.6 15.9 %all-to-all-start.2 = ((bf16[1024,8,32]{0,2,1:T(8,128)(2,1)}), bf16[1024,8,32]{0,2,1:T(8,128)(2,1)S(1)}, u32[]{:S(2)}, u32[]{:S(2)}) async-start(bf16[1024,8,32]{0,2,1:T(8,128)(2,1)} %bitcast.10), calls=%async_computation.3 | async-start | bytes 1048576 | tf_op jit(solution)/shard_map/all_to_all | solution.py:91
  130.5 0.8 copy-start.3
  132.7 14.8 %copy-start.6 = (f32[1024,32]{0,1:T(8,128)S(1)}, f32[1024,32]{0,1:T(8,128)}, u32[]{:S(2)}) copy-start(f32[1024,32]{0,1:T(8,128)} %reduce-scatter.2.cloned.1.call-done) | copy-start | bytes 393220
  133.9 14.7 %copy-start.4 = (bf16[1024,8,32]{0,2,1:T(8,128)(2,1)S(1)}, bf16[1024,8,32]{0,2,1:T(8,128)(2,1)}, u32[]{:S(2)}) copy-start(bf16[1024,8,32]{0,2,1:T(8,128)(2,1)} %copy-done.3) | copy-start | bytes 1572868
  133.9 170.2 %all-to-all-start.3 = ((bf16[64,2,128,32]{2,3,1,0:T(8,128)(2,1)}), bf16[64,2,128,32]{2,3,1,0:T(8,128)(2,1)S(1)}, u32[]{:S(2)}, u32[]{:S(2)}) async-start(bf16[64,2,128,32]{2,3,1,0:T(8,128)(2,1)} %bitcast.110), calls=%async_computation.4 | async-start | bytes 2097152 | tf_op jit(solution)/shard_map/all_to_all | solution.py:122
  147.4 153.9 %all-reduce.6.cloned.1.call-start = ((), (), s32[]{:S(2)}) async-start(), calls=%async_computation.6 | async-start | bytes 131072 | tf_op jit(solution)/shard_map/psum | solution.py:95
  150.4 170.0 %collective-permute-start.2 = (f32[128,32]{0,1:T(8,128)S(1)}, f32[128,32]{0,1:T(8,128)S(1)}, u32[]{:S(2)}, u32[]{:S(2)}) collective-permute-start(f32[128,32]{0,1:T(8,128)S(1)} %get-tuple-element.35), channel_id=1, source_target_pairs={{0,8},{8,16},{16,24},{24,32},{32,40},{40,48},{48,56},{56,64},{64,7... | collective-permute-start | bytes 49160 | tf_op jit(solution)/shard_map/ppermute | solution.py:23
  153.9 166.5 %collective-permute-start.3 = (f32[128,32]{0,1:T(8,128)S(1)}, f32[128,32]{0,1:T(8,128)S(1)}, u32[]{:S(2)}, u32[]{:S(2)}) collective-permute-start(f32[128,32]{0,1:T(8,128)S(1)} %get-tuple-element.34), channel_id=1, source_target_pairs={{8,0},{16,8},{24,16},{32,24},{40,32},{48,40},{56,48},{64,56},{72,6... | collective-permute-start | bytes 49160 | tf_op jit(solution)/shard_map/ppermute | solution.py:23
  320.5 0.7 copy-start.7
Sparse Core Ops, SparseCore 0:
  80.1 28.3 reduce-scatter.1
  152.2 149.0 all-reduce.5
